TPU v7x, 32 devices: a whole 2x2x4 slice. The times are simulated.
32 devices in a mesh: band: 8 (over y, x, core), date: 4 (over z).
Axes of the slice: x: 2, y: 2, z: 4, core: 2. Of those that a mesh axis runs over, the one named last changes fastest.
Arguments:
- inputs: bfloat16 [8, 32, 128, 512], P('date', 'band'), may hold values from -6 to 6
- preact_one: bfloat16 [8, 32, 128, 512], P('date', 'band'), may hold values from -8 to 8
- preact_two: bfloat16 [8, 32, 128, 512], P('date', 'band'), may hold values from -8 to 8
- cotangent: bfloat16 [8, 32, 128, 512], P('date', 'band'), may hold values from -6 to 6
- weight_one: bfloat16 [3, 3, 512, 512], replicated, may hold values from -0.09375 to 0.09375
- weight_two: bfloat16 [3, 3, 512, 512], replicated, may hold values from -0.09375 to 0.09375
Outputs:
- input_grad: bfloat16 [8, 32, 128, 512], P('date', 'band')
- weight_grad_one: float32 [4608, 512], P('date')
- weight_grad_two: float32 [4608, 512], P('date')
All inputs are finite; a program needn't handle non-finite values.
Results may differ from a plain program's by a relative error of at most 0.0057.
Values may be sent and summed in bfloat16 or wider, within the bound.
No kernel may reach another device: no remote copies, remote signals or barrier semaphores. Data moves between devices by JAX's collectives and lax.ppermute only.
A program may use at most 128 MiB of HBM per device.

v0:
```python
import jax
import jax.numpy as jnp
from jax import lax
from jax.sharding import PartitionSpec as P


def extended(array, sides, width):
    for axis, dim in sides:
        peers, length = (lax.axis_size(axis), array.shape[dim])
        up = [(i, (i + 1) % peers) for i in range(peers - 1)]
        down = [(j, i) for i, j in up]
        last = lax.slice_in_dim(array, length - width, length, axis=dim)
        leading = lax.slice_in_dim(array, 0, width, axis=dim)
        before = lax.ppermute(last, axis, up)
        after = lax.ppermute(leading, axis, down)
        array = jnp.concatenate([before, array, after], axis=dim)
    return array


def slope(field_value):
    logistic = jax.nn.sigmoid(field_value)
    return logistic * (1.0 + field_value * (1.0 - logistic))


def pad_columns(field_value):
    return jnp.pad(field_value, ((0, 0), (0, 0), (1, 1), (0, 0)))


def shifted(padded, row_offset, col_offset, row_count, rim_start):
    col_count = padded.shape[2] - 2
    return padded[
        :,
        rim_start - row_offset : rim_start - row_offset + row_count,
        1 - col_offset : 1 - col_offset + col_count,
        :,
    ]


def weight_terms(left_field, padded, rim_start, grad_scale):
    row_count = left_field.shape[1]
    tap_list = []
    for row_offset in (-1, 0, 1):
        for col_offset in (-1, 0, 1):
            shifted_piece = shifted(padded, row_offset, col_offset, row_count, rim_start)
            tap_list.append(
                lax.dot_general(
                    left_field,
                    shifted_piece,
                    (((0, 1, 2), (0, 1, 2)), ((), ())),
                    preferred_element_type=jnp.float32,
                )
            )
    stacked = jnp.stack(tap_list)
    return (stacked * grad_scale).reshape(-1, stacked.shape[2])


def back_terms(padded, weight, row_count, rim_start):
    accumulated = None
    for row_offset in (-1, 0, 1):
        for col_offset in (-1, 0, 1):
            shifted_piece = shifted(padded, row_offset, col_offset, row_count, rim_start)
            product = lax.dot_general(
                shifted_piece,
                weight[row_offset + 1, col_offset + 1],
                (((3,), (1,)), ((), ())),
                preferred_element_type=jnp.float32,
            )
            accumulated = product if accumulated is None else accumulated + product
    return accumulated


def settle(grad_term):
    dates, bands = (lax.axis_size("date"), lax.axis_size("band"))
    rows, cols = grad_term.shape
    piece = rows // (dates * bands)
    by_band = grad_term.reshape(dates, bands, piece, cols).swapaxes(0, 1).reshape(rows, cols)
    share = lax.psum_scatter(by_band, "band", scatter_dimension=0, tiled=True)
    share = lax.psum_scatter(share, "date", scatter_dimension=0, tiled=True)
    return lax.all_gather(share, "band", axis=0, tiled=True)


def body(inputs, preact_one, preact_two, cotangent, weight_one, weight_two):
    row_count = inputs.shape[1]
    grad_scale = 1.0 / (inputs.shape[0] * lax.axis_size("date"))
    act_one = jax.nn.silu(preact_one.astype(jnp.float32)).astype(jnp.bfloat16)
    delta_two = (cotangent.astype(jnp.float32) * slope(preact_two.astype(jnp.float32))).astype(
        jnp.bfloat16
    )
    padded_two = pad_columns(extended(delta_two, (("band", 1),), 1))
    term_two = weight_terms(act_one, padded_two, 1, grad_scale)
    grad_two = settle(term_two)
    back_one = back_terms(padded_two, weight_two, row_count, 1)
    delta_one = (back_one * slope(preact_one.astype(jnp.float32))).astype(jnp.bfloat16)
    padded_one = pad_columns(extended(delta_one, (("band", 1),), 1))
    term_one = weight_terms(inputs, padded_one, 1, grad_scale)
    grad_one = settle(term_one)
    input_grad = back_terms(padded_one, weight_one, row_count, 1).astype(jnp.bfloat16)
    return (input_grad, grad_one, grad_two)


def solution(mesh):
    placed = (
        P("date", "band", None, None),
        P("date", "band", None, None),
        P("date", "band", None, None),
        P("date", "band", None, None),
        P(),
        P(),
    )
    return jax.shard_map(
        body,
        mesh=mesh,
        in_specs=placed,
        out_specs=(P("date", "band", None, None), P("date", None), P("date", None)),
        check_vma=False,
    )
```

profile of v0, /device:TPU:0, one launch (start us, length us, event | category | flops | bytes accessed | tf_op | source)
XLA Modules:
  0.0 340.1 jit_solution(716486030727833753)
XLA Ops:
  7.2 2.5 fusion.7
  9.8 1.4 collective-permute-start.1
  11.2 3.0 collective-permute-start
  14.3 1.1 collective-permute-done
  15.8 2.0 fusion.31
  17.9 1.7 fusion.30
  19.6 1.8 fusion.29
  21.4 2.0 fusion.28
  23.4 1.8 fusion.27
  25.2 1.8 fusion.26
  26.9 2.0 fusion.25
  28.9 1.9 fusion.24
  30.8 1.8 fusion.23
  32.6 4.8 %broadcast_multiply_fusion = f32[9,512,512]{2,1,0:T(8,128)S(1)} fusion(f32[9,512,512]{2,1,0:T(8,128)} %fusion.23), kind=kLoop, calls=%fused_computation.2 | loop fusion | flops 2359296 | bytes 18874368 | tf_op jit(solution)/shard_map/mul | solution.py:54
  37.5 4.8 %copy.28 = f32[8,4,144,512]{3,2,1,0:T(8,128)} copy(f32[8,4,144,512]{3,2,0,1:T(8,128)S(1)} %bitcast.311) | data formatting | bytes 18874368 | tf_op jit(solution)/shard_map/transpose | solution.py:76
  42.5 2.2 fusion.109
  44.8 1.8 fusion.43
  46.7 1.8 fusion.39
  50.0 0.7 fusion.85
  51.5 0.7 fusion.91
  52.7 1.7 fusion.14
  54.5 1.3 collective-permute-start.3
  55.8 7.3 %collective-permute-start.2 = (bf16[2,1,128,512]{3,2,1,0:T(8,128)(2,1)S(1)}, bf16[2,1,128,512]{3,2,1,0:T(8,128)(2,1)S(1)}, u32[]{:S(2)}, u32[]{:S(2)}) collective-permute-start(bf16[2,1,128,512]{3,2,1,0:T(8,128)(2,1)S(1)} %get-tuple-element.4), channel_id=1, source_target_pairs={{0,4},{4,8},{8,12},{12,16},{16,20},{20,24},{24,28},{1,5},{5,9},{9,... | collective-permute-start | bytes 786440 | tf_op jit(solution)/shard_map/ppermute | solution.py:14
  63.1 1.5 collective-permute-done.2
  65.0 1.8 fusion.38
  66.8 1.7 fusion.22
  68.5 1.8 fusion.37
  70.2 1.8 fusion.36
  72.0 1.7 fusion.35
  73.7 1.8 fusion.34
  75.5 1.7 fusion.33
  77.3 1.8 fusion.21
  79.0 1.7 fusion.32
  80.7 5.2 %broadcast_multiply_fusion.1 = f32[9,512,512]{2,1,0:T(8,128)S(1)} fusion(f32[9,512,512]{2,1,0:T(8,128)} %fusion.32), kind=kLoop, calls=%fused_computation.3 | loop fusion | flops 2359296 | bytes 18874368 | tf_op jit(solution)/shard_map/mul | solution.py:54
  85.9 4.7 %copy.18 = f32[8,4,144,512]{3,2,1,0:T(8,128)} copy(f32[8,4,144,512]{3,2,0,1:T(8,128)S(1)} %bitcast.312) | data formatting | bytes 18874368 | tf_op jit(solution)/shard_map/transpose | solution.py:76
  90.7 35.9 %reduce-scatter.9.cloned.1.call-done = f32[576,512]{1,0:T(8,128)} async-done(((f32[4608,512]{1,0:T(8,128)}), f32[576,512]{1,0:T(8,128)}) %reduce-scatter.9.cloned.1.call-update) | async-done | bytes 1179664 | tf_op jit(solution)/shard_map/reduce_scatter | solution.py:77
  126.7 80.0 %reduce-scatter.5.cloned.1.call-done = f32[576,512]{1,0:T(8,128)} async-done(((f32[4608,512]{1,0:T(8,128)}), f32[576,512]{1,0:T(8,128)}) %reduce-scatter.5.cloned.1.call-update) | async-done | bytes 1179664 | tf_op jit(solution)/shard_map/reduce_scatter | solution.py:77
  206.7 31.5 %reduce-scatter.11.cloned.1.call-done = f32[144,512]{1,0:T(8,128)} async-done(((f32[576,512]{1,0:T(8,128)}), f32[144,512]{1,0:T(8,128)}) %reduce-scatter.11.cloned.1.call-update) | async-done | bytes 294928 | tf_op jit(solution)/shard_map/reduce_scatter | solution.py:78
  238.5 29.8 %reduce-scatter.7.cloned.1.call-done = f32[144,512]{1,0:T(8,128)} async-done(((f32[576,512]{1,0:T(8,128)}), f32[144,512]{1,0:T(8,128)}) %reduce-scatter.7.cloned.1.call-update) | async-done | bytes 294928 | tf_op jit(solution)/shard_map/reduce_scatter | solution.py:78
  268.3 2.2 fusion.99
  270.6 1.8 fusion.93
  272.4 1.8 fusion.94
  274.3 0.7 fusion.59
  278.0 2.2 add_convert_fusion
  280.2 17.6 %all-gather.5.cloned.1.call-done = f32[1152,512]{1,0:T(8,128)} async-done(((f32[144,512]{1,0:T(8,128)}), f32[1152,512]{1,0:T(8,128)}) %all-gather.5.cloned.1.call-update) | async-done | bytes 2359312 | tf_op jit(solution)/shard_map/all_gather | solution.py:79
  297.8 30.8 %all-gather.3.cloned.1.call-done = f32[1152,512]{1,0:T(8,128)} async-done(((f32[144,512]{1,0:T(8,128)}), f32[1152,512]{1,0:T(8,128)}) %all-gather.3.cloned.1.call-update) | async-done | bytes 2359312 | tf_op jit(solution)/shard_map/all_gather | solution.py:79
  328.6 3.3 copy.101
  331.8 1.4 copy.102
  (51 shorter events, 7.4 us)
Async XLA Ops:
  7.2 57.8 %copy-start = (bf16[2,4,128,512]{3,2,1,0:T(8,128)(2,1)S(1)}, bf16[2,4,128,512]{3,2,1,0:T(8,128)(2,1)}, u32[]{:S(2)}) copy-start(bf16[2,4,128,512]{3,2,1,0:T(8,128)(2,1)} %param.6) | copy-start | bytes 3145732
  7.2 119.4 %reduce-scatter.9.cloned.1.call-start = ((), (), s32[]{:S(2)}) async-start(), calls=%async_computation.7 | async-start | bytes 10616832 | tf_op jit(solution)/shard_map/reduce_scatter | solution.py:77
  9.7 19.2 %copy-start.3 = (bf16[2,4,128,512]{3,2,1,0:T(8,128)(2,1)}, bf16[2,4,128,512]{3,2,1,0:T(8,128)(2,1)S(1)}, u32[]{:S(2)}) copy-start(bf16[2,4,128,512]{3,2,1,0:T(8,128)(2,1)S(1)} %fusion.7) | copy-start | bytes 3145732
  9.7 6.1 %copy-start.6 = (bf16[2,4,128,512]{3,2,1,0:T(8,128)(2,1)S(1)}, bf16[2,4,128,512]{3,2,1,0:T(8,128)(2,1)}, u32[]{:S(2)}) copy-start(bf16[2,4,128,512]{3,2,1,0:T(8,128)(2,1)} %param.7) | copy-start | bytes 3145732
  9.8 4.5 %collective-permute-start.1 = (bf16[2,1,128,512]{3,2,1,0:T(8,128)(2,1)S(1)}, bf16[2,1,128,512]{3,2,1,0:T(8,128)(2,1)S(1)}, u32[]{:S(2)}, u32[]{:S(2)}) collective-permute-start(bf16[2,1,128,512]{3,2,1,0:T(8,128)(2,1)S(1)} %get-tuple-element.5), channel_id=1, source_target_pairs={{4,0},{8,4},{12,8},{16,12},{20,16},{24,20},{28,24},{5,1},{9,5},{13... | collective-permute-start | bytes 786440 | tf_op jit(solution)/shard_map/ppermute | solution.py:15
  11.2 4.2 %collective-permute-start = (bf16[2,1,128,512]{3,2,1,0:T(8,128)(2,1)S(1)}, bf16[2,1,128,512]{3,2,1,0:T(8,128)(2,1)S(1)}, u32[]{:S(2)}, u32[]{:S(2)}) collective-permute-start(bf16[2,1,128,512]{3,2,1,0:T(8,128)(2,1)S(1)} %get-tuple-element.6), channel_id=1, source_target_pairs={{0,4},{4,8},{8,12},{12,16},{16,20},{20,24},{24,28},{1,5},{5,9},{9,... | collective-permute-start | bytes 786440 | tf_op jit(solution)/shard_map/ppermute | solution.py:14
  42.3 164.4 %reduce-scatter.5.cloned.1.call-start = ((), (), s32[]{:S(2)}) async-start(), calls=%async_computation.4 | async-start | bytes 10616832 | tf_op jit(solution)/shard_map/reduce_scatter | solution.py:77
  42.5 2.3 copy-start.4
  42.5 5.9 %slice-start = ((s8[4718592]{0:T(1024)(128)(4,1)}), s8[4194304]{0:T(1024)(128)(4,1)S(1)}, s32[]{:S(2)}) async-start(s8[4718592]{0:T(1024)(128)(4,1)} %bitcast.313), calls=%async_computation.10 | async-start | bytes 8388608
  44.8 3.7 %slice-start.1 = ((s8[4718592]{0:T(1024)(128)(4,1)}), s8[524288]{0:T(1024)(128)(4,1)S(1)}, s32[]{:S(2)}) async-start(s8[4718592]{0:T(1024)(128)(4,1)} %bitcast.313), calls=%async_computation.11 | async-start | bytes 1048576
  51.5 1.2 copy-start.7
  54.4 22.9 %copy-start.1 = (bf16[2,4,128,512]{3,2,1,0:T(8,128)(2,1)}, bf16[2,4,128,512]{3,2,1,0:T(8,128)(2,1)S(1)}, u32[]{:S(2)}) copy-start(bf16[2,4,128,512]{3,2,1,0:T(8,128)(2,1)S(1)} %fusion.14) | copy-start | bytes 3145732
  54.5 8.6 %collective-permute-start.3 = (bf16[2,1,128,512]{3,2,1,0:T(8,128)(2,1)S(1)}, bf16[2,1,128,512]{3,2,1,0:T(8,128)(2,1)S(1)}, u32[]{:S(2)}, u32[]{:S(2)}) collective-permute-start(bf16[2,1,128,512]{3,2,1,0:T(8,128)(2,1)S(1)} %get-tuple-element.3), channel_id=1, source_target_pairs={{4,0},{8,4},{12,8},{16,12},{20,16},{24,20},{28,24},{5,1},{9,5},{13... | collective-permute-start | bytes 786440 | tf_op jit(solution)/shard_map/ppermute | solution.py:15
  55.8 8.8 %collective-permute-start.2 = (bf16[2,1,128,512]{3,2,1,0:T(8,128)(2,1)S(1)}, bf16[2,1,128,512]{3,2,1,0:T(8,128)(2,1)S(1)}, u32[]{:S(2)}, u32[]{:S(2)}) collective-permute-start(bf16[2,1,128,512]{3,2,1,0:T(8,128)(2,1)S(1)} %get-tuple-element.4), channel_id=1, source_target_pairs={{0,4},{4,8},{8,12},{12,16},{16,20},{20,24},{24,28},{1,5},{5,9},{9,... | collective-permute-start | bytes 786440 | tf_op jit(solution)/shard_map/ppermute | solution.py:14
  90.7 147.5 %reduce-scatter.11.cloned.1.call-start = ((), (), s32[]{:S(2)}) async-start(), calls=%async_computation.8 | async-start | bytes 1474560 | tf_op jit(solution)/shard_map/reduce_scatter | solution.py:78
  126.6 141.6 %reduce-scatter.7.cloned.1.call-start = ((), (), s32[]{:S(2)}) async-start(), calls=%async_computation.5 | async-start | bytes 1474560 | tf_op jit(solution)/shard_map/reduce_scatter | solution.py:78
  206.7 91.1 %all-gather.5.cloned.1.call-start = ((), (), s32[]{:S(2)}) async-start(), calls=%async_computation.9 | async-start | bytes 2654208 | tf_op jit(solution)/shard_map/all_gather | solution.py:79
  238.2 90.3 %all-gather.3.cloned.1.call-start = ((), (), s32[]{:S(2)}) async-start(), calls=%async_computation.6 | async-start | bytes 2654208 | tf_op jit(solution)/shard_map/all_gather | solution.py:79
  268.3 2.3 copy-start.2
  268.3 5.9 %slice-start.2 = ((s8[4718592]{0:T(1024)(128)(4,1)}), s8[4194304]{0:T(1024)(128)(4,1)S(1)}, s32[]{:S(2)}) async-start(s8[4718592]{0:T(1024)(128)(4,1)} %bitcast.315), calls=%async_computation.12 | async-start | bytes 8388608
  270.6 3.7 %slice-start.3 = ((s8[4718592]{0:T(1024)(128)(4,1)}), s8[524288]{0:T(1024)(128)(4,1)S(1)}, s32[]{:S(2)}) async-start(s8[4718592]{0:T(1024)(128)(4,1)} %bitcast.315), calls=%async_computation.13 | async-start | bytes 1048576
  297.8 34.1 %copy-start.5 = (f32[1152,512]{1,0:T(8,128)S(1)}, f32[1152,512]{1,0:T(8,128)}, u32[]{:S(2)}) copy-start(f32[1152,512]{1,0:T(8,128)} %all-gather.5.cloned.1.call-done) | copy-start | bytes 7077892
Sparse Core Ops, SparseCore 0:
  42.4 84.1 reduce-scatter.8
  130.1 76.4 reduce-scatter.4
  209.0 29.1 reduce-scatter.10
  240.4 27.8 reduce-scatter.6
  270.0 27.7 all-gather.4
  299.5 29.0 all-gather.2
where the time goes:
time: 341 us; the launch traced here: 340 us
  waiting for transfers between devices  228 us (67%)
  matrix products  55.6 us (16%)
  local copies, waits for them, and re-layouts  14.8 us (4%)
  between operations  14.5 us (4%)
  starting transfers between devices  13.7 us (4%)
  other arithmetic  13.3 us (4%)
    reduce_scatter x2, waiting for transfers between devices, settle(): share = lax.psum_scatter(by_band, 'band', scatter_dimension=0, tiled=True)  116 us
    reduce_scatter x2, waiting for transfers between devices, settle(): share = lax.psum_scatter(share, 'date', scatter_dimension=0, tiled=True)  61.3 us
    all_gather x2, waiting for transfers between devices, settle(): return lax.all_gather(share, 'band', axis=0, tiled=True)  48.4 us
    dot_general x18, matrix products, weight_terms(): lax.dot_general(left_field, shifted_piece, (((0, 1, 2), (0, 1, 2)), ((),...  32.5 us
    dot_general x18, matrix products, back_terms(): lax.dot_general(shifted_piece, weight[row_offset + 1, col_offset + 1], ((...  23.1 us
    ppermute x2, starting transfers between devices, extended(): before = lax.ppermute(last, axis, up)  10.3 us
    mul x2, other arithmetic, weight_terms(): return (stacked * grad_scale).reshape(-1, stacked.shape[2])  10 us
    transpose x2, local copies, waits for them, and re-layouts, settle(): grad_term.reshape(dates, bands, piece, cols).swapaxes(0, 1)  9.51 us
  transfers between devices with their start and end apart: 10, of which 8 were waited for; matrix products, arithmetic and copies ran while one was open for 14% of the time, Pallas kernels for 0%

commit v1 on v0

--- a/solution.py
+++ b/solution.py
@@ -2,6 +2,24 @@
 import jax.numpy as jnp
 from jax import lax
 from jax.sharding import PartitionSpec as P
+
+
+def ring_gather(value, axis, dim):
+    ways, here, hop = (lax.axis_size(axis), lax.axis_index(axis), value.shape[dim])
+    shape = [n * ways if d == dim else n for d, n in enumerate(value.shape)]
+    full = lax.dynamic_update_slice_in_dim(
+        jnp.zeros(shape, value.dtype), value, here * hop, axis=dim
+    )
+    going_up = going_down = value
+    for far in range(1, ways // 2 + 1):
+        going_up = lax.ppermute(going_up, axis, [(d, (d + 1) % ways) for d in range(ways)])
+        full = lax.dynamic_update_slice_in_dim(full, going_up, (here - far) % ways * hop, axis=dim)
+        if 2 * far < ways:
+            going_down = lax.ppermute(going_down, axis, [(d, (d - 1) % ways) for d in range(ways)])
+            full = lax.dynamic_update_slice_in_dim(
+                full, going_down, (here + far) % ways * hop, axis=dim
+            )
+    return full
 
 
 def extended(array, sides, width):
@@ -76,7 +94,7 @@
     by_band = grad_term.reshape(dates, bands, piece, cols).swapaxes(0, 1).reshape(rows, cols)
     share = lax.psum_scatter(by_band, "band", scatter_dimension=0, tiled=True)
     share = lax.psum_scatter(share, "date", scatter_dimension=0, tiled=True)
-    return lax.all_gather(share, "band", axis=0, tiled=True)
+    return ring_gather(share, "band", 0)
 
 
 def body(inputs, preact_one, preact_two, cotangent, weight_one, weight_two):

time: 341 us -> 319 us (0.935)
  waiting for transfers between devices: 228 us -> 165 us
  matrix products: 55.6 us -> 77.8 us
  starting transfers between devices: 13.7 us -> 29.1 us
  local copies, waits for them, and re-layouts: 14.8 us -> 19.5 us
    all_gather x2 -> x0, waiting for transfers between devices: 48.4 us -> none  [settle(): return lax.all_gather(share, 'band', axis=0, tiled=True)]
    reduce_scatter x2, waiting for transfers between devices: 61.3 us -> 32.2 us  [settle(): share = lax.psum_scatter(share, 'date', scatter_dimension=0, tiled=True)]
    ppermute x0 -> x14, waiting for transfers between devices: none -> 22.7 us  [the longest x8 14.7 us: ring_gather(): lax.ppermute(going_up, axis, [(d, (d + 1) % ways) for d in range(ways)])]
    dot_general x18, matrix products: 23.1 us -> 45.3 us  [back_terms(): lax.dot_general(shifted_piece, weight[row_offset + 1, col_offset + 1], ((...]
    ppermute x0 -> x14, starting transfers between devices: none -> 16.3 us  [the longest x6 16.2 us: ring_gather(): lax.ppermute(going_down, axis, [(d, (d - 1) % ways) for d in range(ways)])]
    reduce_scatter x2, waiting for transfers between devices: 116 us -> 104 us  [settle(): share = lax.psum_scatter(by_band, 'band', scatter_dimension=0, tiled=True)]
    ppermute x2, waiting for transfers between devices: 0.01 us -> 6.11 us  [extended(): after = lax.ppermute(leading, axis, down)]
    dynamic_update_slice x0 -> x16, local copies, waits for them, and re-layouts: none -> 6.06 us  [the longest x8 3.02 us: ring_gather(): lax.dynamic_update_slice_in_dim(full, going_up, (here - far) % ways * hop...]
  transfers between devices with their start and end apart: 10 -> 22, of which waited for: 8 -> 18; matrix products, arithmetic and copies ran while one was open for 14% -> 25% of each run, Pallas kernels for 0% -> 0%
where the time goes in v1:
time: 319 us
  waiting for transfers between devices  165 us (52%)
  matrix products  77.8 us (24%)
  starting transfers between devices  29.1 us (9%)
  local copies, waits for them, and re-layouts  19.5 us (6%)
  between operations  14.3 us (4%)
  other arithmetic  13.2 us (4%)
    reduce_scatter x2, waiting for transfers between devices, settle(): share = lax.psum_scatter(by_band, 'band', scatter_dimension=0, tiled=True)  104 us
    dot_general x18, matrix products, back_terms(): lax.dot_general(shifted_piece, weight[row_offset + 1, col_offset + 1], ((...  45.3 us
    dot_general x18, matrix products, weight_terms(): lax.dot_general(left_field, shifted_piece, (((0, 1, 2), (0, 1, 2)), ((),...  32.5 us
    reduce_scatter x2, waiting for transfers between devices, settle(): share = lax.psum_scatter(share, 'date', scatter_dimension=0, tiled=True)  32.2 us
    ppermute x6, starting transfers between devices, ring_gather(): lax.ppermute(going_down, axis, [(d, (d - 1) % ways) for d in range(ways)])  16.2 us
    ppermute x8, waiting for transfers between devices, ring_gather(): lax.ppermute(going_up, axis, [(d, (d + 1) % ways) for d in range(ways)])  14.7 us
    mul x2, other arithmetic, weight_terms(): return (stacked * grad_scale).reshape(-1, stacked.shape[2])  9.92 us
    transpose x2, local copies, waits for them, and re-layouts, settle(): grad_term.reshape(dates, bands, piece, cols).swapaxes(0, 1)  9.47 us
  transfers between devices with their start and end apart: 22, of which 18 were waited for; matrix products, arithmetic and copies ran while one was open for 25% of the time, Pallas kernels for 0%

profile of v1, /device:TPU:0, one launch (start us, length us, event | category | flops | bytes accessed | tf_op | source)
XLA Modules:
  0.0 318.7 jit_solution(2365844800977032444)
XLA Ops:
  7.2 2.5 fusion.7
  9.8 2.5 collective-permute-start
  13.6 4.2 %collective-permute-done.1 = bf16[2,1,128,512]{3,2,1,0:T(8,128)(2,1)S(1)} collective-permute-done((bf16[2,1,128,512]{3,2,1,0:T(8,128)(2,1)S(1)}, bf16[2,1,128,512]{3,2,1,0:T(8,128)(2,1)S(1)}, u32[]{:S(2)}, u32[]{:S(2)}) %collective-permute-start.1) | collective-permute-done | bytes 262176 | tf_op jit(solution)/shard_map/ppermute | solution.py:33
  18.2 2.0 fusion.31
  20.3 1.8 fusion.30
  22.0 1.8 fusion.29
  23.8 2.0 fusion.28
  25.8 1.8 fusion.27
  27.6 1.8 fusion.26
  29.4 2.0 fusion.25
  31.4 1.9 fusion.24
  33.2 1.8 fusion.23
  35.0 4.8 %broadcast_multiply_fusion = f32[9,512,512]{2,1,0:T(8,128)S(1)} fusion(f32[9,512,512]{2,1,0:T(8,128)} %fusion.23), kind=kLoop, calls=%fused_computation.2 | loop fusion | flops 2359296 | bytes 18874368 | tf_op jit(solution)/shard_map/mul | solution.py:72
  39.9 4.8 %copy.28 = f32[8,4,144,512]{3,2,1,0:T(8,128)} copy(f32[8,4,144,512]{3,2,0,1:T(8,128)S(1)} %bitcast.311) | data formatting | bytes 18874368 | tf_op jit(solution)/shard_map/transpose | solution.py:94
  45.0 2.2 fusion.109
  47.3 1.8 fusion.39
  49.1 1.8 fusion.43
  56.9 6.9 %collective-permute-start.2 = (bf16[2,1,128,512]{3,2,1,0:T(8,128)(2,1)S(1)}, bf16[2,1,128,512]{3,2,1,0:T(8,128)(2,1)S(1)}, u32[]{:S(2)}, u32[]{:S(2)}) collective-permute-start(bf16[2,1,128,512]{3,2,1,0:T(8,128)(2,1)S(1)} %get-tuple-element.4), channel_id=1, source_target_pairs={{0,4},{4,8},{8,12},{12,16},{16,20},{20,24},{24,28},{1,5},{5,9},{9,... | collective-permute-start | bytes 786440 | tf_op jit(solution)/shard_map/ppermute | solution.py:32
  65.4 1.9 collective-permute-done.3
  69.4 1.8 fusion.22
  72.9 1.8 fusion.36
  74.7 1.8 fusion.35
  81.7 1.8 fusion.32
  83.4 5.1 %broadcast_multiply_fusion.1 = f32[9,512,512]{2,1,0:T(8,128)S(1)} fusion(f32[9,512,512]{2,1,0:T(8,128)} %fusion.32), kind=kLoop, calls=%fused_computation.3 | loop fusion | flops 2359296 | bytes 18874368 | tf_op jit(solution)/shard_map/mul | solution.py:72
  88.5 4.6 %copy.18 = f32[8,4,144,512]{3,2,1,0:T(8,128)} copy(f32[8,4,144,512]{3,2,0,1:T(8,128)S(1)} %bitcast.312) | data formatting | bytes 18874368 | tf_op jit(solution)/shard_map/transpose | solution.py:94
  93.2 33.8 %reduce-scatter.9.cloned.1.call-done = f32[576,512]{1,0:T(8,128)} async-done(((f32[4608,512]{1,0:T(8,128)}), f32[576,512]{1,0:T(8,128)}) %reduce-scatter.9.cloned.1.call-update) | async-done | bytes 1179664 | tf_op jit(solution)/shard_map/reduce_scatter | solution.py:95
  127.5 3.5 %fusion.99 = f32[2,4,128,512]{3,2,1,0:T(8,128)} fusion(bf16[2,4,128,512]{3,2,1,0:T(8,128)(2,1)} %copy-done.1, bf16[3,3,512,512]{3,2,1,0:T(8,128)(2,1)} %param.10), kind=kOutput, calls=%fused_computation.127 | convolution fusion | flops 536870912 | bytes 3670016 | tf_op jit(solution)/shard_map/dot_general | solution.py:80
  131.0 3.1 fusion.94
  134.1 3.1 fusion.59
  137.3 69.8 %reduce-scatter.5.cloned.1.call-done = f32[576,512]{1,0:T(8,128)} async-done(((f32[4608,512]{1,0:T(8,128)}), f32[576,512]{1,0:T(8,128)}) %reduce-scatter.5.cloned.1.call-update) | async-done | bytes 1179664 | tf_op jit(solution)/shard_map/reduce_scatter | solution.py:95
  207.1 3.3 %fusion.93 = f32[2,4,128,512]{3,2,1,0:T(8,128)} fusion(bf16[2,4,128,512]{3,2,1,0:T(8,128)(2,1)} %copy-done.1, bf16[2,1,128,512]{3,2,1,0:T(8,128)(2,1)S(1)} %collective-permute-done.2, bf16[3,3,512,512]{3,2,1,0:T(8,128)(2,1)} %param.10), kind=kOutput, calls=%fused_computation.121 | convolution fusion | flops 539492352 | bytes 3932160 | tf_op jit(solution)/shard_map/dot_general | solution.py:80
  210.4 3.1 fusion.62
  213.5 3.2 fusion.65
  216.7 3.2 fusion.68
  219.9 3.1 fusion.71
  223.0 15.6 %reduce-scatter.11.cloned.1.call-done = f32[144,512]{1,0:T(8,128)} async-done(((f32[576,512]{1,0:T(8,128)}), f32[144,512]{1,0:T(8,128)}) %reduce-scatter.11.cloned.1.call-update) | async-done | bytes 294928 | tf_op jit(solution)/shard_map/reduce_scatter | solution.py:96
  238.6 2.6 collective-permute-start.12
  241.2 8.4 %add_convert_fusion = bf16[2,4,128,512]{3,2,1,0:T(8,128)(2,1)} fusion(f32[2,4,128,512]{3,2,1,0:T(8,128)} %fusion.93, f32[2,4,128,512]{3,2,1,0:T(8,128)} %fusion.59, f32[2,4,128,512]{3,2,1,0:T(8,128)} %fusion.62, f32[2,4,128,512]{3,2,1,0:T(8,128)} %fusion.99, f32[2,4,128,512]{3,2,1,0:T(8,128)} %fusion.65, f32[2,4,128,512]{3,2,1,0:T(8,128)} %fusion.68, ...), kind=kOutput, calls=%fused_computation.25 | convolution fusion | flops 541589504 | bytes 19398656 | tf_op jit(solution)/shard_map/dot_general | solution.py:80
  252.1 16.6 %reduce-scatter.7.cloned.1.call-done = f32[144,512]{1,0:T(8,128)} async-done(((f32[576,512]{1,0:T(8,128)}), f32[144,512]{1,0:T(8,128)}) %reduce-scatter.7.cloned.1.call-update) | async-done | bytes 294928 | tf_op jit(solution)/shard_map/reduce_scatter | solution.py:96
  268.7 2.6 collective-permute-start.5
  271.8 2.6 collective-permute-start.14
  277.3 1.8 collective-permute-done.5
  279.1 2.7 collective-permute-start.7
  285.3 2.8 collective-permute-start.16
  291.6 2.8 collective-permute-start.9
  298.7 3.9 %collective-permute-done.8 = f32[144,512]{1,0:T(8,128)S(1)} collective-permute-done((f32[144,512]{1,0:T(8,128)S(1)}, f32[144,512]{1,0:T(8,128)S(1)}, u32[]{:S(2)}, u32[]{:S(2)}) %collective-permute-start.8) | collective-permute-done | bytes 294944 | tf_op jit(solution)/shard_map/ppermute | solution.py:15
  304.3 3.2 %collective-permute-done.17 = f32[144,512]{1,0:T(8,128)S(1)} collective-permute-done((f32[144,512]{1,0:T(8,128)S(1)}, f32[144,512]{1,0:T(8,128)S(1)}, u32[]{:S(2)}, u32[]{:S(2)}) %collective-permute-start.17) | collective-permute-done | bytes 294944 | tf_op jit(solution)/shard_map/ppermute | solution.py:15
  308.3 2.4 collective-permute-done.10
  (88 shorter events, 39.9 us)
Async XLA Ops:
  7.2 60.5 %copy-start = (bf16[2,4,128,512]{3,2,1,0:T(8,128)(2,1)S(1)}, bf16[2,4,128,512]{3,2,1,0:T(8,128)(2,1)}, u32[]{:S(2)}) copy-start(bf16[2,4,128,512]{3,2,1,0:T(8,128)(2,1)} %param.6) | copy-start | bytes 3145732
  7.2 119.9 %reduce-scatter.9.cloned.1.call-start = ((), (), s32[]{:S(2)}) async-start(), calls=%async_computation.6 | async-start | bytes 10616832 | tf_op jit(solution)/shard_map/reduce_scatter | solution.py:95
  9.7 21.7 %copy-start.3 = (bf16[2,4,128,512]{3,2,1,0:T(8,128)(2,1)}, bf16[2,4,128,512]{3,2,1,0:T(8,128)(2,1)S(1)}, u32[]{:S(2)}) copy-start(bf16[2,4,128,512]{3,2,1,0:T(8,128)(2,1)S(1)} %fusion.7) | copy-start | bytes 3145732
  9.7 8.5 %copy-start.6 = (bf16[2,4,128,512]{3,2,1,0:T(8,128)(2,1)S(1)}, bf16[2,4,128,512]{3,2,1,0:T(8,128)(2,1)}, u32[]{:S(2)}) copy-start(bf16[2,4,128,512]{3,2,1,0:T(8,128)(2,1)} %param.7) | copy-start | bytes 3145732
  9.8 3.8 %collective-permute-start = (bf16[2,1,128,512]{3,2,1,0:T(8,128)(2,1)S(1)}, bf16[2,1,128,512]{3,2,1,0:T(8,128)(2,1)S(1)}, u32[]{:S(2)}, u32[]{:S(2)}) collective-permute-start(bf16[2,1,128,512]{3,2,1,0:T(8,128)(2,1)S(1)} %get-tuple-element.6), channel_id=1, source_target_pairs={{0,4},{4,8},{8,12},{12,16},{16,20},{20,24},{24,28},{1,5},{5,9},{9,... | collective-permute-start | bytes 786440 | tf_op jit(solution)/shard_map/ppermute | solution.py:32
  12.3 5.5 %collective-permute-start.1 = (bf16[2,1,128,512]{3,2,1,0:T(8,128)(2,1)S(1)}, bf16[2,1,128,512]{3,2,1,0:T(8,128)(2,1)S(1)}, u32[]{:S(2)}, u32[]{:S(2)}) collective-permute-start(bf16[2,1,128,512]{3,2,1,0:T(8,128)(2,1)S(1)} %get-tuple-element.5), channel_id=1, source_target_pairs={{4,0},{8,4},{12,8},{16,12},{20,16},{24,20},{28,24},{5,1},{9,5},{13... | collective-permute-start | bytes 786440 | tf_op jit(solution)/shard_map/ppermute | solution.py:33
  44.8 162.3 %reduce-scatter.5.cloned.1.call-start = ((), (), s32[]{:S(2)}) async-start(), calls=%async_computation.4 | async-start | bytes 10616832 | tf_op jit(solution)/shard_map/reduce_scatter | solution.py:95
  45.0 2.3 copy-start.4
  45.0 5.9 %slice-start = ((s8[4718592]{0:T(1024)(128)(4,1)}), s8[4194304]{0:T(1024)(128)(4,1)S(1)}, s32[]{:S(2)}) async-start(s8[4718592]{0:T(1024)(128)(4,1)} %bitcast.313), calls=%async_computation.8 | async-start | bytes 8388608
  47.3 3.6 %slice-start.1 = ((s8[4718592]{0:T(1024)(128)(4,1)}), s8[524288]{0:T(1024)(128)(4,1)S(1)}, s32[]{:S(2)}) async-start(s8[4718592]{0:T(1024)(128)(4,1)} %bitcast.313), calls=%async_computation.9 | async-start | bytes 1048576
  53.9 1.2 copy-start.7
  56.9 23.1 %copy-start.1 = (bf16[2,4,128,512]{3,2,1,0:T(8,128)(2,1)}, bf16[2,4,128,512]{3,2,1,0:T(8,128)(2,1)S(1)}, u32[]{:S(2)}) copy-start(bf16[2,4,128,512]{3,2,1,0:T(8,128)(2,1)S(1)} %fusion.14) | copy-start | bytes 3145732
  56.9 8.4 %collective-permute-start.2 = (bf16[2,1,128,512]{3,2,1,0:T(8,128)(2,1)S(1)}, bf16[2,1,128,512]{3,2,1,0:T(8,128)(2,1)S(1)}, u32[]{:S(2)}, u32[]{:S(2)}) collective-permute-start(bf16[2,1,128,512]{3,2,1,0:T(8,128)(2,1)S(1)} %get-tuple-element.4), channel_id=1, source_target_pairs={{0,4},{4,8},{8,12},{12,16},{16,20},{20,24},{24,28},{1,5},{5,9},{9,... | collective-permute-start | bytes 786440 | tf_op jit(solution)/shard_map/ppermute | solution.py:32
  63.8 3.4 %collective-permute-start.3 = (bf16[2,1,128,512]{3,2,1,0:T(8,128)(2,1)S(1)}, bf16[2,1,128,512]{3,2,1,0:T(8,128)(2,1)S(1)}, u32[]{:S(2)}, u32[]{:S(2)}) collective-permute-start(bf16[2,1,128,512]{3,2,1,0:T(8,128)(2,1)S(1)} %get-tuple-element.3), channel_id=1, source_target_pairs={{4,0},{8,4},{12,8},{16,12},{20,16},{24,20},{28,24},{5,1},{9,5},{13... | collective-permute-start | bytes 786440 | tf_op jit(solution)/shard_map/ppermute | solution.py:33
  93.2 145.4 %reduce-scatter.11.cloned.1.call-start = ((), (), s32[]{:S(2)}) async-start(), calls=%async_computation.7 | async-start | bytes 1474560 | tf_op jit(solution)/shard_map/reduce_scatter | solution.py:96
  127.1 141.6 %reduce-scatter.7.cloned.1.call-start = ((), (), s32[]{:S(2)}) async-start(), calls=%async_computation.5 | async-start | bytes 1474560 | tf_op jit(solution)/shard_map/reduce_scatter | solution.py:96
  127.5 3.5 %copy-start.2 = (bf16[2,4,128,512]{3,2,1,0:T(8,128)(2,1)S(1)}, bf16[2,4,128,512]{3,2,1,0:T(8,128)(2,1)}, u32[]{:S(2)}) copy-start(bf16[2,4,128,512]{3,2,1,0:T(8,128)(2,1)} %copy-done.1) | copy-start | bytes 3145732
  238.6 33.1 %collective-permute-start.11 = (f32[144,512]{1,0:T(8,128)}, f32[144,512]{1,0:T(8,128)S(1)}, u32[]{:S(2)}, u32[]{:S(2)}) collective-permute-start(f32[144,512]{1,0:T(8,128)} %reduce-scatter.11.cloned.1.call-done), channel_id=1, source_target_pairs={{0,4},{4,8},{8,12},{12,16},{16,20},{20,24},{24,28},{28,0},{1,5},{5... | collective-permute-start | bytes 884744 | tf_op jit(solution)/shard_map/ppermute | solution.py:15
  238.6 33.2 %collective-permute-start.12 = (f32[144,512]{1,0:T(8,128)}, f32[144,512]{1,0:T(8,128)S(1)}, u32[]{:S(2)}, u32[]{:S(2)}) collective-permute-start(f32[144,512]{1,0:T(8,128)} %reduce-scatter.11.cloned.1.call-done), channel_id=1, source_target_pairs={{0,28},{4,0},{8,4},{12,8},{16,12},{20,16},{24,20},{28,24},{1,29},{... | collective-permute-start | bytes 884744 | tf_op jit(solution)/shard_map/ppermute | solution.py:18
  249.6 1.7 copy-start.8
  268.7 2.9 copy-start.9
  268.7 8.6 %collective-permute-start.4 = (f32[144,512]{1,0:T(8,128)}, f32[144,512]{1,0:T(8,128)S(1)}, u32[]{:S(2)}, u32[]{:S(2)}) collective-permute-start(f32[144,512]{1,0:T(8,128)} %reduce-scatter.7.cloned.1.call-done), channel_id=1, source_target_pairs={{0,4},{4,8},{8,12},{12,16},{16,20},{20,24},{24,28},{28,0},{1,5},{5... | collective-permute-start | bytes 884744 | tf_op jit(solution)/shard_map/ppermute | solution.py:15
  268.7 10.4 %collective-permute-start.5 = (f32[144,512]{1,0:T(8,128)}, f32[144,512]{1,0:T(8,128)S(1)}, u32[]{:S(2)}, u32[]{:S(2)}) collective-permute-start(f32[144,512]{1,0:T(8,128)} %reduce-scatter.7.cloned.1.call-done), channel_id=1, source_target_pairs={{0,28},{4,0},{8,4},{12,8},{16,12},{20,16},{24,20},{28,24},{1,29},{... | collective-permute-start | bytes 884744 | tf_op jit(solution)/shard_map/ppermute | solution.py:18
  271.7 11.9 %collective-permute-start.13 = (f32[144,512]{1,0:T(8,128)S(1)}, f32[144,512]{1,0:T(8,128)S(1)}, u32[]{:S(2)}, u32[]{:S(2)}) collective-permute-start(f32[144,512]{1,0:T(8,128)S(1)} %collective-permute-done.11), channel_id=1, source_target_pairs={{0,4},{4,8},{8,12},{12,16},{16,20},{20,24},{24,28},{28,0},{1,5},{5... | collective-permute-start | bytes 884744 | tf_op jit(solution)/shard_map/ppermute | solution.py:15
  271.8 13.6 %collective-permute-start.14 = (f32[144,512]{1,0:T(8,128)S(1)}, f32[144,512]{1,0:T(8,128)S(1)}, u32[]{:S(2)}, u32[]{:S(2)}) collective-permute-start(f32[144,512]{1,0:T(8,128)S(1)} %collective-permute-done.12), channel_id=1, source_target_pairs={{0,28},{4,0},{8,4},{12,8},{16,12},{20,16},{24,20},{28,24},{1,29},{... | collective-permute-start | bytes 884744 | tf_op jit(solution)/shard_map/ppermute | solution.py:18
  277.3 12.6 %collective-permute-start.6 = (f32[144,512]{1,0:T(8,128)S(1)}, f32[144,512]{1,0:T(8,128)S(1)}, u32[]{:S(2)}, u32[]{:S(2)}) collective-permute-start(f32[144,512]{1,0:T(8,128)S(1)} %collective-permute-done.4), channel_id=1, source_target_pairs={{0,4},{4,8},{8,12},{12,16},{16,20},{20,24},{24,28},{28,0},{1,5},{5... | collective-permute-start | bytes 884744 | tf_op jit(solution)/shard_map/ppermute | solution.py:15
  279.1 12.5 %collective-permute-start.7 = (f32[144,512]{1,0:T(8,128)S(1)}, f32[144,512]{1,0:T(8,128)S(1)}, u32[]{:S(2)}, u32[]{:S(2)}) collective-permute-start(f32[144,512]{1,0:T(8,128)S(1)} %collective-permute-done.5), channel_id=1, source_target_pairs={{0,28},{4,0},{8,4},{12,8},{16,12},{20,16},{24,20},{28,24},{1,29},{... | collective-permute-start | bytes 884744 | tf_op jit(solution)/shard_map/ppermute | solution.py:18
  283.6 12.6 %collective-permute-start.15 = (f32[144,512]{1,0:T(8,128)S(1)}, f32[144,512]{1,0:T(8,128)S(1)}, u32[]{:S(2)}, u32[]{:S(2)}) collective-permute-start(f32[144,512]{1,0:T(8,128)S(1)} %collective-permute-done.13), channel_id=1, source_target_pairs={{0,4},{4,8},{8,12},{12,16},{16,20},{20,24},{24,28},{28,0},{1,5},{5... | collective-permute-start | bytes 884744 | tf_op jit(solution)/shard_map/ppermute | solution.py:15
  285.3 12.6 %collective-permute-start.16 = (f32[144,512]{1,0:T(8,128)S(1)}, f32[144,512]{1,0:T(8,128)S(1)}, u32[]{:S(2)}, u32[]{:S(2)}) collective-permute-start(f32[144,512]{1,0:T(8,128)S(1)} %collective-permute-done.14), channel_id=1, source_target_pairs={{0,28},{4,0},{8,4},{12,8},{16,12},{20,16},{24,20},{28,24},{1,29},{... | collective-permute-start | bytes 884744 | tf_op jit(solution)/shard_map/ppermute | solution.py:18
  289.9 12.6 %collective-permute-start.8 = (f32[144,512]{1,0:T(8,128)S(1)}, f32[144,512]{1,0:T(8,128)S(1)}, u32[]{:S(2)}, u32[]{:S(2)}) collective-permute-start(f32[144,512]{1,0:T(8,128)S(1)} %collective-permute-done.6), channel_id=1, source_target_pairs={{0,4},{4,8},{8,12},{12,16},{16,20},{20,24},{24,28},{28,0},{1,5},{5... | collective-permute-start | bytes 884744 | tf_op jit(solution)/shard_map/ppermute | solution.py:15
  291.6 12.6 %collective-permute-start.9 = (f32[144,512]{1,0:T(8,128)S(1)}, f32[144,512]{1,0:T(8,128)S(1)}, u32[]{:S(2)}, u32[]{:S(2)}) collective-permute-start(f32[144,512]{1,0:T(8,128)S(1)} %collective-permute-done.7), channel_id=1, source_target_pairs={{0,28},{4,0},{8,4},{12,8},{16,12},{20,16},{24,20},{28,24},{1,29},{... | collective-permute-start | bytes 884744 | tf_op jit(solution)/shard_map/ppermute | solution.py:18
  296.2 11.3 %collective-permute-start.17 = (f32[144,512]{1,0:T(8,128)S(1)}, f32[144,512]{1,0:T(8,128)S(1)}, u32[]{:S(2)}, u32[]{:S(2)}) collective-permute-start(f32[144,512]{1,0:T(8,128)S(1)} %collective-permute-done.15), channel_id=1, source_target_pairs={{0,4},{4,8},{8,12},{12,16},{16,20},{20,24},{24,28},{28,0},{1,5},{5... | collective-permute-start | bytes 884744 | tf_op jit(solution)/shard_map/ppermute | solution.py:15
  302.6 8.1 %collective-permute-start.10 = (f32[144,512]{1,0:T(8,128)S(1)}, f32[144,512]{1,0:T(8,128)S(1)}, u32[]{:S(2)}, u32[]{:S(2)}) collective-permute-start(f32[144,512]{1,0:T(8,128)S(1)} %collective-permute-done.8), channel_id=1, source_target_pairs={{0,4},{4,8},{8,12},{12,16},{16,20},{20,24},{24,28},{28,0},{1,5},{5... | collective-permute-start | bytes 884744 | tf_op jit(solution)/shard_map/ppermute | solution.py:15
  310.7 1.4 copy-start.5
Sparse Core Ops, SparseCore 0:
  44.9 82.1 reduce-scatter.8
  130.5 76.4 reduce-scatter.4
  209.4 29.1 reduce-scatter.10
  240.8 27.8 reduce-scatter.6
